TPU v7x, 128 devices: a whole 4x4x4 slice. The times are simulated.
128 devices in a mesh: row: 16 (over y, x_hi, core), col: 8 (over x_lo, z).
Axes of the slice: x: 4 (x_hi: 2, x_lo: 2; x = x_hi * 2 + x_lo), y: 4, z: 4, core: 2. Of those that a mesh axis runs over, the one named last changes fastest.
Arguments:
- matrix: float32 [24576, 4, 3072], P('row', None, 'col'), may hold values from -60 to 60, as said below
Outputs:
- factored: float32 [24576, 4, 3072], P('row', None, 'col')
- r_rows: float32 [2, 384, 4, 3072], P(None, None, None, 'col')
Inputs may be any that keep to these rules, and one draw needn't show every extreme that they name: `matrix`: dense real entries with column scales that differ from column to column.
All inputs are finite; a program needn't handle non-finite values.
Results may differ from a plain program's by a relative error of at most 0.00017.
Values sent between devices are 32-bit elements; how exact they have to be, the bound alone decides.
No kernel may reach another device: no remote copies, remote signals or barrier semaphores. Data moves between devices by JAX's collectives and lax.ppermute only.
A program may use at most 128 MiB of HBM per device.

v0:
```python
import jax
import jax.numpy as jnp
from jax import lax
from jax.sharding import PartitionSpec as P

STEPS = 2


def spread(block, axis, holder):
    block = jnp.where(lax.axis_index(axis) == holder, block, jnp.zeros_like(block))
    return lax.psum(block, axis)


def shards(matrix):
    highest = lax.Precision.HIGHEST
    ncol = lax.axis_size("col")
    column = lax.axis_index("col")
    count = matrix.shape[1]
    width = matrix.shape[2]
    glob = jnp.arange(count, dtype=jnp.int32) * ncol + column
    ident = jnp.eye(width, dtype=jnp.float32)
    blocks = matrix
    rows_out = []
    for k in range(STEPS):
        owner = k % ncol
        local_index = k // ncol
        local_panel = blocks[:, local_index, :]
        gram = lax.psum(
            jnp.dot(
                local_panel.T, local_panel, precision=highest, preferred_element_type=jnp.float32
            ),
            "row",
        )
        lower = jnp.linalg.cholesky(gram)
        inverse = lax.linalg.triangular_solve(lower, ident, left_side=True, lower=True)
        own_basis = jnp.dot(
            local_panel, inverse.T, precision=highest, preferred_element_type=jnp.float32
        )
        basis = spread(own_basis, "col", owner)
        partial_proj = jnp.einsum("mb,mjt->bjt", basis, blocks, precision=highest)
        proj = lax.psum(partial_proj, "row")
        kept = jnp.where((glob > k)[None, :, None], proj, jnp.float32(0.0))
        blocks = blocks - jnp.einsum("mb,bjt->mjt", basis, kept, precision=highest)
        is_panel = (glob == k)[None, :, None]
        blocks = jnp.where(is_panel, basis[:, None, :], blocks)
        rows_out.append(jnp.where(is_panel, lower.T[:, None, :], kept))
    return (blocks, jnp.stack(rows_out))


def solution(mesh):
    return jax.shard_map(
        shards,
        mesh=mesh,
        in_specs=(P("row", None, "col"),),
        out_specs=(P("row", None, "col"), P(None, None, None, "col")),
        check_vma=False,
    )
```

profile of v0, /device:TPU:0, one launch (start us, length us, event | category | flops | bytes accessed | tf_op | source)
XLA Modules:
  0.0 1087.4 jit_solution(16035788120656499901)
XLA Ops:
  7.2 4.3 copy.16
  11.5 3.7 copy-done.1
  15.2 4.8 fusion.7
  20.7 141.6 %all-reduce.8.cloned.1.call-done = f32[384,384]{0,1:T(8,128)} async-done(((f32[384,384]{0,1:T(8,128)}), f32[384,384]{0,1:T(8,128)}) %all-reduce.8.cloned.1.call-update) | async-done | bytes 589840 | tf_op jit(solution)/shard_map/psum | solution.py:28
  162.3 1.3 copy.18
  163.6 1.1 fusion.26
  164.7 11.7 %cholesky.208 = f32[128,128]{1,0:T(8,128)S(1)} custom-call(f32[128,128]{1,0:T(8,128)S(1)} %cholesky.310), custom_call_target="Cholesky" | custom-call | tf_op jit(solution)/shard_map/jit(cholesky)/cholesky | solution.py:34
  176.4 9.8 custom-call.20
  186.9 11.7 %cholesky.227 = f32[128,128]{1,0:T(8,128)S(1)} custom-call(f32[128,128]{1,0:T(8,128)S(1)} %cholesky.314), custom_call_target="Cholesky" | custom-call | tf_op jit(solution)/shard_map/jit(cholesky)/cholesky | solution.py:34
  198.6 10.0 custom-call.21
  209.1 11.7 %cholesky.246 = f32[128,128]{1,0:T(8,128)S(1)} custom-call(f32[128,128]{1,0:T(8,128)S(1)} %convolution_subtract_fusion.7), custom_call_target="Cholesky" | custom-call | tf_op jit(solution)/shard_map/jit(cholesky)/cholesky | solution.py:34
  224.2 6.4 while.4
  224.9 1.4 bitcast_dynamic-update-slice_fusion.4
  227.0 1.4 bitcast_dynamic-update-slice_fusion.4
  229.1 1.4 bitcast_dynamic-update-slice_fusion.4
  230.6 29.5 %custom-call.22 = f32[3,128,128]{1,2,0:T(8,128)S(1)} custom-call(f32[3,128,128]{2,1,0:T(8,128)S(1)} %get-tuple-element.18), custom_call_target="InvertDiagBlocksLowerTriangular" | custom-call | tf_op jit(solution)/shard_map/triangular_solve/custom-call.2 | solution.py:35
  261.9 7.0 fusion
  269.0 81.4 %all-reduce.10.cloned.1.call-done = f32[1536,384]{0,1:T(8,128)} async-done(((f32[1536,384]{0,1:T(8,128)}), f32[1536,384]{0,1:T(8,128)}) %all-reduce.10.cloned.1.call-update) | async-done | bytes 2359312 | tf_op jit(solution)/shard_map/psum | solution.py:11
  350.4 16.7 %fusion.4 = f32[384,4,384]{2,0,1:T(8,128)} fusion(f32[1536,384]{0,1:T(8,128)} %all-reduce.10.cloned.1.call-done, f32[1536,4,384]{2,1,0:T(4,128)} %param.4), kind=kOutput, calls=%fused_computation.15 | convolution fusion | flops 10871635968 | bytes 14155776 | tf_op jit(solution)/shard_map/mb,mjt->bjt/dot_general | solution.py:40
  367.2 2.0 copy.19
  369.3 145.5 %all-reduce.12.cloned.1.call-done = f32[384,4,384]{2,0,1:T(8,128)} async-done(((f32[384,4,384]{2,0,1:T(8,128)}), f32[384,4,384]{2,0,1:T(8,128)}) %all-reduce.12.cloned.1.call-update) | async-done | bytes 2359312 | tf_op jit(solution)/shard_map/psum | solution.py:41
  514.8 21.5 %subtract_select_fusion.1 = f32[1536,4,384]{2,0,1:T(8,128)S(1)} fusion(f32[1536,384]{1,0:T(8,128)S(1)} %copy.19, pred[4]{0:T(512)(128)(4,1)S(1)} %get-tuple-element.67, f32[1536,384]{0,1:T(8,128)} %all-reduce.10.cloned.1.call-done, f32[384,4,384]{2,0,1:T(8,128)} %all-reduce.12.cloned.1.call-done, pred[4]{0:T(512)(128)(4,1)S(1)} %get-tuple-element.66, ...), kind=kOutput, calls=%fused_computation.5 | convolution fusion | flops 10876944384 | bytes 25952264 | tf_op jit(solution)/shard_map/mb,bjt->mjt/dot_general | solution.py:43
  536.4 3.7 copy-done
  540.1 4.8 fusion.8
  545.0 139.8 %all-reduce.14.cloned.1.call-done = f32[384,384]{0,1:T(8,128)} async-done(((f32[384,384]{0,1:T(8,128)}), f32[384,384]{0,1:T(8,128)}) %all-reduce.14.cloned.1.call-update) | async-done | bytes 589840 | tf_op jit(solution)/shard_map/psum | solution.py:28
  684.8 1.3 copy.24
  686.1 1.1 fusion.25
  687.3 11.7 %cholesky.261 = f32[128,128]{1,0:T(8,128)S(1)} custom-call(f32[128,128]{1,0:T(8,128)S(1)} %cholesky.318), custom_call_target="Cholesky" | custom-call | tf_op jit(solution)/shard_map/jit(cholesky)/cholesky | solution.py:34
  699.7 9.8 custom-call.23
  710.1 11.7 %cholesky.280 = f32[128,128]{1,0:T(8,128)S(1)} custom-call(f32[128,128]{1,0:T(8,128)S(1)} %cholesky.322), custom_call_target="Cholesky" | custom-call | tf_op jit(solution)/shard_map/jit(cholesky)/cholesky | solution.py:34
  722.5 10.2 custom-call.24
  733.2 11.7 %cholesky.299 = f32[128,128]{1,0:T(8,128)S(1)} custom-call(f32[128,128]{1,0:T(8,128)S(1)} %convolution_subtract_fusion.6), custom_call_target="Cholesky" | custom-call | tf_op jit(solution)/shard_map/jit(cholesky)/cholesky | solution.py:34
  748.3 6.1 while.5
  749.0 1.4 bitcast_dynamic-update-slice_fusion.5
  751.0 1.4 bitcast_dynamic-update-slice_fusion.5
  753.1 1.4 bitcast_dynamic-update-slice_fusion.5
  754.5 29.5 %custom-call.25 = f32[3,128,128]{1,2,0:T(8,128)S(1)} custom-call(f32[3,128,128]{2,1,0:T(8,128)S(1)} %get-tuple-element.19), custom_call_target="InvertDiagBlocksLowerTriangular" | custom-call | tf_op jit(solution)/shard_map/triangular_solve/custom-call.2 | solution.py:35
  785.8 6.9 convolution_select_fusion
  792.8 81.4 %all-reduce.16.cloned.1.call-done = f32[1536,384]{1,0:T(8,128)} async-done(((f32[1536,384]{1,0:T(8,128)}), f32[1536,384]{1,0:T(8,128)}) %all-reduce.16.cloned.1.call-update) | async-done | bytes 2359312 | tf_op jit(solution)/shard_map/psum | solution.py:11
  874.2 16.2 %fusion.1 = f32[384,4,384]{2,0,1:T(8,128)} fusion(f32[1536,4,384]{2,0,1:T(8,128)} %copy-done, f32[1536,384]{1,0:T(8,128)} %all-reduce.16.cloned.1.call-done), kind=kOutput, calls=%fused_computation.12 | convolution fusion | flops 10871635968 | bytes 14155776 | tf_op jit(solution)/shard_map/mb,mjt->bjt/dot_general | solution.py:40
  890.5 1.0 copy.26
  892.3 2.8 select_bitcast_fusion.1
  895.3 142.8 %all-reduce.18.cloned.1.call-done = f32[384,4,384]{2,0,1:T(8,128)} async-done(((f32[384,4,384]{2,0,1:T(8,128)}), f32[384,4,384]{2,0,1:T(8,128)}) %all-reduce.18.cloned.1.call-update) | async-done | bytes 2359312 | tf_op jit(solution)/shard_map/psum | solution.py:41
  1038.1 2.1 select_bitcast_fusion
  1040.8 5.4 copy.29
  1046.3 1.1 copy-done.4
  1047.4 16.5 %subtract_select_fusion = f32[1536,4,384]{2,0,1:T(8,128)S(1)} fusion(f32[1536,4,384]{2,0,1:T(8,128)S(1)} %bitcast.110, f32[1536,384]{1,0:T(8,128)S(1)} %copy-done.2, pred[4]{0:T(512)(128)(4,1)S(1)} %get-tuple-element.69, f32[384,4,384]{2,0,1:T(8,128)S(1)} %copy-done.4, pred[4]{0:T(512)(128)(4,1)S(1)} %get-tuple-element.68), kind=kOutput, calls=%fused_computation.4 | convolution fusion | flops 10876944384 | bytes 23592968 | tf_op jit(solution)/shard_map/mb,bjt->mjt/dot_general | solution.py:43
  1063.9 16.5 %copy.28 = f32[1536,4,384]{2,1,0:T(4,128)} copy(f32[1536,4,384]{2,0,1:T(8,128)S(1)} %subtract_select_fusion) | data formatting | bytes 18874368
  (88 shorter events, 16.8 us)
Async XLA Ops:
  7.2 155.1 %all-reduce.8.cloned.1.call-start = ((), (), s32[]{:S(2)}) async-start(), calls=%async_computation | async-start | bytes 1179648 | tf_op jit(solution)/shard_map/psum | solution.py:28
  11.5 3.7 copy-start.1
  20.1 330.3 %all-reduce.10.cloned.1.call-start = ((), (), s32[]{:S(2)}) async-start(), calls=%async_computation.1 | async-start | bytes 4718592 | tf_op jit(solution)/shard_map/psum | solution.py:11
  268.9 245.9 %all-reduce.12.cloned.1.call-start = ((), (), s32[]{:S(2)}) async-start(), calls=%async_computation.2 | async-start | bytes 4718592 | tf_op jit(solution)/shard_map/psum | solution.py:41
  367.2 317.7 %all-reduce.14.cloned.1.call-start = ((), (), s32[]{:S(2)}) async-start(), calls=%async_computation.3 | async-start | bytes 1179648 | tf_op jit(solution)/shard_map/psum | solution.py:28
  536.4 3.7 copy-start
  545.0 329.2 %all-reduce.16.cloned.1.call-start = ((), (), s32[]{:S(2)}) async-start(), calls=%async_computation.4 | async-start | bytes 4718592 | tf_op jit(solution)/shard_map/psum | solution.py:11
  792.8 245.4 %all-reduce.18.cloned.1.call-start = ((), (), s32[]{:S(2)}) async-start(), calls=%async_computation.5 | async-start | bytes 4718592 | tf_op jit(solution)/shard_map/psum | solution.py:41
  890.4 1.9 copy-start.3
  892.3 2.8 copy-start.6
  1038.1 2.4 copy-start.5
  1040.5 5.8 slice-start
  1040.5 5.8 slice-start.1
  1040.8 5.5 slice-start.2
  1040.8 5.5 copy-start.2
  1040.8 6.6 copy-start.4
Sparse Core Ops, SparseCore 0:
  20.2 141.9 all-reduce.7
  269.1 81.3 all-reduce.9
  367.3 147.4 all-reduce.11
  545.1 139.7 all-reduce.13
  792.9 81.2 all-reduce.15
  890.6 147.5 all-reduce.17
where the time goes:
time: 1090 us
  waiting for transfers between devices  733 us (67%)
  other arithmetic  181 us (17%)
  matrix products  100 us (9%)
  local copies, waits for them, and re-layouts  54.3 us (5%)
  between operations  18.5 us (2%)
    psum x2, waiting for transfers between devices, shards(): proj = lax.psum(partial_proj, 'row')  288 us
    psum x2, waiting for transfers between devices, shards(): lax.psum(jnp.dot(local_panel.T, local_panel, precision=highest, preferred...  281 us
    psum x2, waiting for transfers between devices, spread(): return lax.psum(block, axis)  163 us
    another operation x21, other arithmetic, shards(): lower = jnp.linalg.cholesky(gram)  114 us
    another operation x3, other arithmetic, shards(): lax.linalg.triangular_solve(lower, ident, left_side=True, lower=True)  59 us
    dot_general x2, matrix products, shards(): blocks = blocks - jnp.einsum('mb,bjt->mjt', basis, kept, precision=highest)  38 us
    unnamed x23, local copies, waits for them, and re-layouts  35.9 us
    dot_general x2, matrix products, shards(): partial_proj = jnp.einsum('mb,mjt->bjt', basis, blocks, precision=highest)  32.9 us
  transfers between devices with their start and end apart: 6, of which 6 were waited for; matrix products, arithmetic and copies ran while one was open for 1% of the time, Pallas kernels for 0%

commit v1 on v0

--- a/solution.py
+++ b/solution.py
@@ -8,7 +8,7 @@
 
 def spread(block, axis, holder):
     block = jnp.where(lax.axis_index(axis) == holder, block, jnp.zeros_like(block))
-    return lax.psum(block, axis)
+    return jnp.sum(lax.all_gather(block, axis), axis=0)
 
 
 def shards(matrix):

time: 1090 us -> 1330 us (1.22)
  waiting for transfers between devices: 733 us -> 943 us
  local copies, waits for them, and re-layouts: 54.3 us -> 74 us
    all_gather x0 -> x2, waiting for transfers between devices: none -> 376 us  [spread(): return jnp.sum(lax.all_gather(block, axis), axis=0)]
    psum x2 -> x0, waiting for transfers between devices: 163 us -> none  [spread(): return lax.psum(block, axis)]
    unnamed x23 -> x28, local copies, waits for them, and re-layouts: 35.9 us -> 55.2 us
where the time goes in v1:
time: 1330 us
  waiting for transfers between devices  943 us (71%)
  other arithmetic  194 us (15%)
  matrix products  95.8 us (7%)
  local copies, waits for them, and re-layouts  74 us (6%)
  between operations  18.7 us (1%)
    all_gather x2, waiting for transfers between devices, spread(): return jnp.sum(lax.all_gather(block, axis), axis=0)  376 us
    psum x2, waiting for transfers between devices, shards(): proj = lax.psum(partial_proj, 'row')  287 us
    psum x2, waiting for transfers between devices, shards(): lax.psum(jnp.dot(local_panel.T, local_panel, precision=highest, preferred...  281 us
    another operation x21, other arithmetic, shards(): lower = jnp.linalg.cholesky(gram)  114 us
    another operation x3, other arithmetic, shards(): lax.linalg.triangular_solve(lower, ident, left_side=True, lower=True)  59 us
    unnamed x28, local copies, waits for them, and re-layouts  55.2 us
    dot_general x2, matrix products, shards(): blocks = blocks - jnp.einsum('mb,bjt->mjt', basis, kept, precision=highest)  38.1 us
    dot_general x2, matrix products, shards(): partial_proj = jnp.einsum('mb,mjt->bjt', basis, blocks, precision=highest)  28.5 us
  transfers between devices with their start and end apart: 6, of which 6 were waited for; matrix products, arithmetic and copies ran while one was open for 1% of the time, Pallas kernels for 0%

profile of v1, /device:TPU:0, one launch (start us, length us, event | category | flops | bytes accessed | tf_op | source)
XLA Modules:
  0.0 1327.6 jit_solution(4765655790008969531)
XLA Ops:
  7.2 4.3 copy.28
  11.5 3.7 copy-done.2
  15.2 4.8 fusion.7
  20.7 141.6 %all-reduce.6.cloned.1.call-done = f32[384,384]{0,1:T(8,128)} async-done(((f32[384,384]{0,1:T(8,128)}), f32[384,384]{0,1:T(8,128)}) %all-reduce.6.cloned.1.call-update) | async-done | bytes 589840 | tf_op jit(solution)/shard_map/psum | solution.py:28
  162.3 1.3 copy.30
  164.7 11.7 cholesky.208
  176.4 9.8 custom-call.20
  186.9 11.7 cholesky.227
  198.6 10.0 custom-call.21
  209.1 11.7 cholesky.246
  224.2 6.4 while.4
  224.9 1.4 bitcast_dynamic-update-slice_fusion.4
  227.0 1.4 bitcast_dynamic-update-slice_fusion.4
  229.1 1.4 bitcast_dynamic-update-slice_fusion.4
  230.6 29.5 %custom-call.22 = f32[3,128,128]{1,2,0:T(8,128)S(1)} custom-call(f32[3,128,128]{2,1,0:T(8,128)S(1)} %get-tuple-element.18), custom_call_target="InvertDiagBlocksLowerTriangular" | custom-call | tf_op jit(solution)/shard_map/triangular_solve/custom-call.2 | solution.py:35
  261.9 7.0 fusion
  269.0 187.8 %all-gather.5.cloned.1.call-done = f32[12288,384]{0,1:T(8,128)} async-done(((f32[1536,384]{0,1:T(8,128)}), f32[12288,384]{0,1:T(8,128)}) %all-gather.5.cloned.1.call-update) | async-done | bytes 18874384 | tf_op jit(solution)/shard_map/all_gather | solution.py:11
  456.8 20.0 %copy.48 = f32[48,8,8,1536]{3,2,1,0:T(8,128)S(1)} copy(f32[48,8,8,1536]{3,1,2,0:T(8,128)} %bitcast.120) | data formatting | bytes 37748736
  476.8 5.2 bitcast_reduce_fusion
  482.1 1.4 copy-done.1
  483.5 13.0 fusion.4
  496.5 2.2 copy.31
  498.7 144.6 %all-reduce.8.cloned.1.call-done = f32[384,4,384]{2,0,1:T(8,128)} async-done(((f32[384,4,384]{2,0,1:T(8,128)}), f32[384,4,384]{2,0,1:T(8,128)}) %all-reduce.8.cloned.1.call-update) | async-done | bytes 2359312 | tf_op jit(solution)/shard_map/psum | solution.py:41
  643.3 21.4 %subtract_select_fusion.1 = f32[1536,4,384]{2,0,1:T(8,128)S(1)} fusion(f32[1536,384]{1,0:T(8,128)S(1)} %copy.31, pred[4]{0:T(512)(128)(4,1)S(1)} %get-tuple-element.69, f32[1536,384]{0,1:T(8,128)} %copy-done.1, f32[384,4,384]{2,0,1:T(8,128)} %all-reduce.8.cloned.1.call-done, pred[4]{0:T(512)(128)(4,1)S(1)} %get-tuple-element.68, f32[1536,4,384]{2,1,0:T(4,128)} %param.4), kind=kOutput, calls=%fused_computation.6 | convolution fusion | flops 10876944384 | bytes 25952264 | tf_op jit(solution)/shard_map/mb,bjt->mjt/dot_general | solution.py:43
  664.7 3.7 copy-done
  668.4 4.8 fusion.8
  673.5 139.6 %all-reduce.10.cloned.1.call-done = f32[384,384]{0,1:T(8,128)} async-done(((f32[384,384]{0,1:T(8,128)}), f32[384,384]{0,1:T(8,128)}) %all-reduce.10.cloned.1.call-update) | async-done | bytes 589840 | tf_op jit(solution)/shard_map/psum | solution.py:28
  813.1 1.3 copy.36
  815.6 11.7 cholesky.261
  827.4 9.8 custom-call.23
  837.8 11.7 cholesky.280
  850.9 10.2 custom-call.24
  861.5 11.7 cholesky.299
  876.7 6.4 while.5
  877.4 1.4 bitcast_dynamic-update-slice_fusion.5
  879.5 1.4 bitcast_dynamic-update-slice_fusion.5
  881.7 1.4 bitcast_dynamic-update-slice_fusion.5
  883.1 29.5 %custom-call.25 = f32[3,128,128]{1,2,0:T(8,128)S(1)} custom-call(f32[3,128,128]{2,1,0:T(8,128)S(1)} %get-tuple-element.19), custom_call_target="InvertDiagBlocksLowerTriangular" | custom-call | tf_op jit(solution)/shard_map/triangular_solve/custom-call.2 | solution.py:35
  914.5 6.9 convolution_select_fusion
  921.6 187.7 %all-gather.7.cloned.1.call-done = f32[12288,384]{1,0:T(8,128)} async-done(((f32[1536,384]{1,0:T(8,128)}), f32[12288,384]{1,0:T(8,128)}) %all-gather.7.cloned.1.call-update) | async-done | bytes 18874384 | tf_op jit(solution)/shard_map/all_gather | solution.py:11
  1109.3 7.5 reduce_sum.19
  1116.9 15.5 %fusion.1 = f32[384,4,384]{2,0,1:T(8,128)} fusion(f32[1536,4,384]{2,0,1:T(8,128)} %copy-done, f32[1536,384]{1,0:T(8,128)S(1)} %reduce_sum.19), kind=kOutput, calls=%fused_computation.13 | convolution fusion | flops 10871635968 | bytes 14155776 | tf_op jit(solution)/shard_map/mb,mjt->bjt/dot_general | solution.py:40
  1133.5 3.5 select_bitcast_fusion.1
  1137.2 142.1 %all-reduce.12.cloned.1.call-done = f32[384,4,384]{2,0,1:T(8,128)} async-done(((f32[384,4,384]{2,0,1:T(8,128)}), f32[384,4,384]{2,0,1:T(8,128)}) %all-reduce.12.cloned.1.call-update) | async-done | bytes 2359312 | tf_op jit(solution)/shard_map/psum | solution.py:41
  1279.3 2.1 select_bitcast_fusion
  1282.0 5.2 copy.41
  1287.2 16.8 %subtract_select_fusion = f32[1536,4,384]{2,0,1:T(8,128)S(1)} fusion(f32[1536,4,384]{2,0,1:T(8,128)S(1)} %bitcast.116, f32[1536,384]{1,0:T(8,128)S(1)} %reduce_sum.19, pred[4]{0:T(512)(128)(4,1)S(1)} %get-tuple-element.71, f32[384,4,384]{2,0,1:T(8,128)S(1)} %copy-done.3, pred[4]{0:T(512)(128)(4,1)S(1)} %get-tuple-element.70), kind=kOutput, calls=%fused_computation.5 | convolution fusion | flops 10876944384 | bytes 23592968 | tf_op jit(solution)/shard_map/mb,bjt->mjt/dot_general | solution.py:43
  1304.0 16.5 %copy.40 = f32[1536,4,384]{2,1,0:T(4,128)} copy(f32[1536,4,384]{2,0,1:T(8,128)S(1)} %subtract_select_fusion) | data formatting | bytes 18874368
  (96 shorter events, 19.8 us)
Async XLA Ops:
  7.2 155.1 %all-reduce.6.cloned.1.call-start = ((), (), s32[]{:S(2)}) async-start(), calls=%async_computation | async-start | bytes 1179648 | tf_op jit(solution)/shard_map/psum | solution.py:28
  11.5 3.7 copy-start.2
  20.1 436.7 %all-gather.5.cloned.1.call-start = ((), (), s32[]{:S(2)}) async-start(), calls=%async_computation.4 | async-start | bytes 21233664 | tf_op jit(solution)/shard_map/all_gather | solution.py:11
  268.9 374.4 %all-reduce.8.cloned.1.call-start = ((), (), s32[]{:S(2)}) async-start(), calls=%async_computation.1 | async-start | bytes 4718592 | tf_op jit(solution)/shard_map/psum | solution.py:41
  456.8 26.6 %slice-start.3 = ((s8[9437184]{0:T(1024)(128)(4,1)}), s8[4194304]{0:T(1024)(128)(4,1)S(1)}, s32[]{:S(2)}) async-start(s8[9437184]{0:T(1024)(128)(4,1)} %bitcast.117), calls=%async_computation.9 | async-start | bytes 8388608
  456.8 26.6 %slice-start.4 = ((s8[9437184]{0:T(1024)(128)(4,1)}), s8[4194304]{0:T(1024)(128)(4,1)S(1)}, s32[]{:S(2)}) async-start(s8[9437184]{0:T(1024)(128)(4,1)} %bitcast.117), calls=%async_computation.10 | async-start | bytes 8388608
  476.8 6.6 slice-start.5
  482.1 1.4 copy-start.1
  496.5 316.7 %all-reduce.10.cloned.1.call-start = ((), (), s32[]{:S(2)}) async-start(), calls=%async_computation.2 | async-start | bytes 1179648 | tf_op jit(solution)/shard_map/psum | solution.py:28
  664.7 3.7 copy-start
  673.3 436.0 %all-gather.7.cloned.1.call-start = ((), (), s32[]{:S(2)}) async-start(), calls=%async_computation.5 | async-start | bytes 21233664 | tf_op jit(solution)/shard_map/all_gather | solution.py:11
  921.4 357.8 %all-reduce.12.cloned.1.call-start = ((), (), s32[]{:S(2)}) async-start(), calls=%async_computation.3 | async-start | bytes 4718592 | tf_op jit(solution)/shard_map/psum | solution.py:41
  1133.5 3.5 copy-start.5
  1279.3 2.4 copy-start.4
  1281.6 5.6 slice-start
  1281.6 5.6 slice-start.1
  1282.0 5.3 slice-start.2
  1282.0 5.2 copy-start.3
Sparse Core Ops, SparseCore 0:
  20.2 141.9 all-reduce.5
  269.1 187.7 all-gather.4
  496.6 146.6 all-reduce.7
  673.4 139.6 all-reduce.9
  921.5 187.7 all-gather.6
  1132.5 146.6 all-reduce.11
